TPU v7x, 32 devices: a whole 2x2x4 slice. The times are simulated.
32 devices in a mesh: dp: 2 (over core), ctx: 16 (over z, y, x).
Axes of the slice: x: 2, y: 2, z: 4, core: 2. Of those that a mesh axis runs over, the one named last changes fastest.
Arguments:
- tokens: bfloat16 [8192, 2880], P(('dp', 'ctx')), parts along dimension 0, may hold values from -6 to 6
- positions: int32 [8192], P(('dp', 'ctx')), parts along dimension 0, may hold values from 0 to 4223, as said below
- norm_gain: float32 [2880], replicated, may hold values from 0.5 to 1.5
- qkv_weight: bfloat16 [2880, 2560], P(None, 'ctx'), may hold values from -4 to 4
- qkv_bias: float32 [2560], replicated, may hold values from -3 to 3
- sinks: float32 [32], replicated, may hold values from 0 to 4
- earlier_keys: bfloat16 [256, 256], P('dp'), parts along dimension 0, may hold values from -6 to 6
- earlier_values: bfloat16 [256, 256], P('dp'), parts along dimension 0, may hold values from -6 to 6
Outputs:
- attended: bfloat16 [8192, 2048], P(('dp', 'ctx')), parts along dimension 0
There are 2 independent parts, one for each index of `dp`. A program takes and returns all parts, laid end to end along the dimension named above; an argument that names none is the same for every part. Nothing has to cross between parts.
Inputs may be any that keep to these rules, and one draw needn't show every extreme that they name: Within each document positions rise by one from token to token and restart at 0 where the next document begins; the first token of the span continues a document of the previous span and has position 128 or more, so that the previous span's last 128 tokens belong to it; at least one document begins inside the span, and the token just before the first such start has position 4223.
All inputs are finite; a program needn't handle non-finite values.
Results may differ from a plain program's by a relative error of at most 0.0074.
Values may be sent and summed in bfloat16 or wider, within the bound.
No kernel may reach another device: no remote copies, remote signals or barrier semaphores. Data moves between devices by JAX's collectives and lax.ppermute only.
A program may use at most 64 MiB of HBM per device.

v0:
```python
import jax
import jax.numpy as jnp
from jax import lax
from jax.sharding import PartitionSpec as P

QUERY_HEADS = 32
KEY_VALUE_HEADS = 4
HEAD_SIZE = 64
WINDOW_TOKENS = 128


def shifted(value, axis, steps):
    count = lax.axis_size(axis)
    leading, last = (max(0, -steps), min(count, count - steps))
    return lax.ppermute(value, axis, [(source, source + steps) for source in range(leading, last)])


def apply_rotation(heads, positions):
    half = heads.shape[-1] // 2
    freq = 150000.0 ** (-(jnp.arange(half, dtype=jnp.float32) * 2.0 / heads.shape[-1]))
    angle = positions.astype(jnp.float32)[:, None] * freq[None, :]
    cosine = jnp.cos(angle)[:, None, :]
    sine = jnp.sin(angle)[:, None, :]
    first = heads[..., :half]
    second = heads[..., half:]
    return jnp.concatenate(
        [first * cosine - second * sine, second * cosine + first * sine], axis=-1
    )


def attend_head(query_rows, key_rows, value_rows, sink_row, visible):
    scores = jnp.einsum(
        "nrgd,nkd->ngrk", query_rows, key_rows, preferred_element_type=jnp.float32
    ) * HEAD_SIZE ** (-0.5)
    scores = jnp.where(visible[:, None], scores, -1e30)
    top = jnp.maximum(jnp.max(scores, axis=-1), sink_row[None, :, None])
    expo = jnp.exp(scores - top[..., None])
    total = jnp.sum(expo, axis=-1) + jnp.exp(sink_row[None, :, None] - top)
    probs = (expo / total[..., None]).astype(jnp.bfloat16)
    out = jnp.einsum("ngrk,nkd->nrgd", probs, value_rows, preferred_element_type=jnp.float32)
    return out.astype(jnp.bfloat16)


def send_rim(window_output, token_rows):
    return shifted(window_output[:, token_rows - WINDOW_TOKENS :], "ctx", 1)


def split_mixed(combined_output, positions, token_rows, query_length, key_length):
    key_rows = apply_rotation(
        combined_output[:, query_length : query_length + key_length].reshape(
            token_rows, KEY_VALUE_HEADS, HEAD_SIZE
        ),
        positions,
    ).astype(jnp.bfloat16)
    value_rows = combined_output[:, query_length + key_length :].astype(jnp.bfloat16)
    window_output = jnp.stack([key_rows.reshape(token_rows, key_length), value_rows])
    received = send_rim(window_output, token_rows)
    query_rows = apply_rotation(
        combined_output[:, :query_length].reshape(token_rows, QUERY_HEADS, HEAD_SIZE), positions
    ).astype(jnp.bfloat16)
    return (window_output, received, query_rows)


def on_device(
    tokens, positions, norm_gain, qkv_weight, qkv_bias, sinks, earlier_keys, earlier_values
):
    token_rows = tokens.shape[0]
    query_group = QUERY_HEADS // KEY_VALUE_HEADS
    query_length = QUERY_HEADS * HEAD_SIZE
    key_length = KEY_VALUE_HEADS * HEAD_SIZE
    flat = tokens.astype(jnp.float32)
    scale = lax.rsqrt(jnp.mean(flat * flat, axis=-1, keepdims=True) + 1e-05)
    normed = (flat * scale * norm_gain[None, :]).astype(jnp.bfloat16)
    combined_output = jnp.dot(
        normed,
        lax.all_gather(qkv_weight, "ctx", axis=1, tiled=True),
        preferred_element_type=jnp.float32,
    )
    combined_output = combined_output + qkv_bias[None, :]
    window_output, received, query_rows = split_mixed(
        combined_output, positions, token_rows, query_length, key_length
    )
    prior = jnp.stack([earlier_keys, earlier_values])
    border_tokens = jnp.where(lax.axis_index("ctx") == 0, prior, received)
    padded_rows = jnp.concatenate([border_tokens, window_output], axis=1).reshape(
        2, WINDOW_TOKENS + token_rows, KEY_VALUE_HEADS, HEAD_SIZE
    )
    joined_keys = padded_rows[0]
    joined_values = padded_rows[1]
    limit = jnp.minimum(positions, WINDOW_TOKENS - 1)
    sink_tokens = sinks.reshape(KEY_VALUE_HEADS, query_group)
    rel = (
        jnp.arange(token_rows, dtype=jnp.int32)[:, None]
        - jnp.arange(WINDOW_TOKENS + token_rows, dtype=jnp.int32)[None, :]
        + WINDOW_TOKENS
    )
    visible = ((rel >= 0) & (rel <= limit[:, None]))[None]
    query_blocks = query_rows.reshape(1, token_rows, KEY_VALUE_HEADS, query_group, HEAD_SIZE)
    window_keys = joined_keys[None]
    window_values = joined_values[None]

    def one_head(items):
        return attend_head(items[0], items[1], items[2], items[3], visible)

    out = lax.map(
        one_head,
        (
            jnp.moveaxis(query_blocks, 2, 0),
            jnp.moveaxis(window_keys, 2, 0),
            jnp.moveaxis(window_values, 2, 0),
            sink_tokens,
        ),
    )
    return jnp.moveaxis(out, 0, 2).reshape(token_rows, query_length)


def solution(mesh):
    placed = (
        P(("dp", "ctx"), None),
        P(("dp", "ctx")),
        P(),
        P(None, "ctx"),
        P(),
        P(),
        P("dp", None),
        P("dp", None),
    )
    return jax.shard_map(
        on_device, mesh=mesh, in_specs=placed, out_specs=P(("dp", "ctx"), None), check_vma=False
    )
```

profile of v0, /device:TPU:4, one launch (start us, length us, event | category | flops | bytes accessed | tf_op | source)
XLA Modules:
  0.0 232.4 jit_solution(17536291176751203206)
XLA Ops:
  6.5 0.7 all-gather.2.cloned.1.call-update
  7.3 0.7 reshape.219
  8.0 1.8 fusion.30
  9.8 0.8 broadcast_minimum_fusion
  10.6 0.8 multiply_cosine_fusion
  11.4 175.5 %all-gather.2.cloned.1.call-done = bf16[2880,2560]{0,1:T(8,128)(2,1)} async-done(((bf16[2880,160]{0,1:T(8,128)(2,1)}), bf16[2880,2560]{0,1:T(8,128)(2,1)}) %all-gather.2.cloned.1.call-update) | async-done | bytes 14745616 | tf_op jit(solution)/shard_map/all_gather | solution.py:76
  187.0 9.2 %convolution_add_fusion = f32[256,2560]{1,0:T(8,128)S(1)} fusion(bf16[2880,2560]{0,1:T(8,128)(2,1)} %all-gather.2.cloned.1.call-done, bf16[256,2880]{0,1:T(8,128)(2,1)} %param.10, f32[2880]{0:T(1024)} %param.12, f32[256]{0:T(256)S(1)} %add_rsqrt_fusion, f32[2560]{0:T(1024)} %param.14), kind=kOutput, calls=%fused_computation.30 | convolution fusion | flops 3778478080 | bytes 18864384 | tf_op jit(solution)/shard_map/dot_general | solution.py:74
  196.2 1.5 slice.55
  197.7 1.9 copy.20
  199.8 1.1 subtract_convert_fusion
  200.9 0.8 subtract_convert_fusion.1
  201.9 2.5 %collective-permute-start = (bf16[2,128,256]{2,1,0:T(8,128)(2,1)S(1)}, bf16[2,128,256]{2,1,0:T(8,128)(2,1)S(1)}, u32[]{:S(2)}, u32[]{:S(2)}) collective-permute-start(bf16[2,128,256]{2,1,0:T(8,128)(2,1)S(1)} %pad_maximum_fusion), channel_id=1, source_target_pairs={{0,1},{1,2},{2,3},{3,4},{4,5},{5,6},{6,7},{7,8},{8,9},{9,10},{10,1... | collective-permute-start | bytes 393224 | tf_op jit(solution)/shard_map/ppermute | solution.py:15
  204.5 5.2 %collective-permute-done = bf16[2,128,256]{2,1,0:T(8,128)(2,1)S(1)} collective-permute-done((bf16[2,128,256]{2,1,0:T(8,128)(2,1)S(1)}, bf16[2,128,256]{2,1,0:T(8,128)(2,1)S(1)}, u32[]{:S(2)}, u32[]{:S(2)}) %collective-permute-start) | collective-permute-done | bytes 131104 | tf_op jit(solution)/shard_map/ppermute | solution.py:15
  210.1 13.2 %while.11 = (s32[]{:T(128)}, bf16[4,1,256,8,64]{2,4,3,1,0:T(8,128)(2,1)}, bf16[4,1,384,64]{2,3,1,0:T(8,128)(2,1)S(1)}, bf16[4,1,384,64]{2,3,1,0:T(8,128)(2,1)S(1...) while((s32[]{:T(128)}, ...), condition=%wide.region_4.5_spmd.clone, body=%wide.region_1.4_spmd.clone.sunk | while | flops 211390464 | bytes 10538209 | solution.py:105
  210.2 0.7 fusion.49
  211.7 1.7 fusion.52
  213.5 0.7 fusion.49
  214.3 0.7 fusion.51
  215.0 1.7 fusion.52
  216.8 0.7 fusion.49
  218.3 1.7 fusion.52
  220.1 0.7 fusion.49
  221.6 1.7 fusion.52
  223.3 2.3 copy.26
  (39 shorter events, 3.8 us)
Async XLA Ops:
  6.5 180.4 %all-gather.2.cloned.1.call-start = ((), (), s32[]{:S(2)}) async-start(), calls=%async_computation | async-start | bytes 16015360 | tf_op jit(solution)/shard_map/all_gather | solution.py:76
  200.9 8.8 %copy-start = (bf16[128,256]{1,0:T(8,128)(2,1)S(1)}, bf16[128,256]{1,0:T(8,128)(2,1)}, u32[]{:S(2)}) copy-start(bf16[128,256]{1,0:T(8,128)(2,1)} %param.17) | copy-start | bytes 196612
  200.9 8.8 %copy-start.1 = (bf16[128,256]{1,0:T(8,128)(2,1)S(1)}, bf16[128,256]{1,0:T(8,128)(2,1)}, u32[]{:S(2)}) copy-start(bf16[128,256]{1,0:T(8,128)(2,1)} %param.16) | copy-start | bytes 196612
  201.9 7.8 %collective-permute-start = (bf16[2,128,256]{2,1,0:T(8,128)(2,1)S(1)}, bf16[2,128,256]{2,1,0:T(8,128)(2,1)S(1)}, u32[]{:S(2)}, u32[]{:S(2)}) collective-permute-start(bf16[2,128,256]{2,1,0:T(8,128)(2,1)S(1)} %pad_maximum_fusion), channel_id=1, source_target_pairs={{0,1},{1,2},{2,3},{3,4},{4,5},{5,6},{6,7},{7,8},{8,9},{9,10},{10,1... | collective-permute-start | bytes 393224 | tf_op jit(solution)/shard_map/ppermute | solution.py:15
Sparse Core Ops, SparseCore 0:
  10.1 176.7 all-gather.1
where the time goes:
time: 233 us; the launch traced here: 232 us
  waiting for transfers between devices  181 us (78%)
  matrix products  18.7 us (8%)
  between operations  13.5 us (6%)
  other arithmetic  9.07 us (4%)
  local copies, waits for them, and re-layouts  7.09 us (3%)
  starting transfers between devices  2.47 us (1%)
    all_gather x1, waiting for transfers between devices, on_device(): lax.all_gather(qkv_weight, 'ctx', axis=1, tiled=True)  176 us
    dot_general x1, matrix products, on_device(): jnp.dot(normed, lax.all_gather(qkv_weight, 'ctx', axis=1, tiled=True), pr...  9.19 us
    dot_general x4, matrix products, attend_head(): jnp.einsum('ngrk,nkd->nrgd', probs, value_rows, preferred_element_type=jn...  6.84 us
    ppermute x1, waiting for transfers between devices, shifted(): lax.ppermute(value, axis, [(source, source + steps) for source in range(l...  5.2 us
  transfers between devices with their start and end apart: 2, of which 2 were waited for; matrix products, arithmetic and copies ran while one was open for 2% of the time, Pallas kernels for 0%

commit v1 on v0

--- a/solution.py
+++ b/solution.py
@@ -7,6 +7,27 @@
 KEY_VALUE_HEADS = 4
 HEAD_SIZE = 64
 WINDOW_TOKENS = 128
+
+
+def gather_around(value, axis, dim):
+    size, place, span = (lax.axis_size(axis), lax.axis_index(axis), value.shape[dim])
+    ahead = [(i, (i + 1) % size) for i in range(size)]
+    left = [(i, (i - 1) % size) for i in range(size)]
+    out = jnp.zeros((*value.shape[:dim], size * span, *value.shape[dim + 1 :]), value.dtype)
+    out = lax.dynamic_update_slice_in_dim(out, value, place * span, axis=dim)
+    from_left = from_right = value
+    middle = size // 2
+    for step in range(1, middle + 1):
+        from_left = lax.ppermute(from_left, axis, ahead)
+        out = lax.dynamic_update_slice_in_dim(
+            out, from_left, (place - step) % size * span, axis=dim
+        )
+        if step < size - middle:
+            from_right = lax.ppermute(from_right, axis, left)
+            out = lax.dynamic_update_slice_in_dim(
+                out, from_right, (place + step) % size * span, axis=dim
+            )
+    return out
 
 
 def shifted(value, axis, steps):
@@ -72,9 +93,7 @@
     scale = lax.rsqrt(jnp.mean(flat * flat, axis=-1, keepdims=True) + 1e-05)
     normed = (flat * scale * norm_gain[None, :]).astype(jnp.bfloat16)
     combined_output = jnp.dot(
-        normed,
-        lax.all_gather(qkv_weight, "ctx", axis=1, tiled=True),
-        preferred_element_type=jnp.float32,
+        normed, gather_around(qkv_weight, "ctx", 1), preferred_element_type=jnp.float32
     )
     combined_output = combined_output + qkv_bias[None, :]
     window_output, received, query_rows = split_mixed(

time: 233 us -> 352 us (1.51)
  waiting for transfers between devices: 181 us -> 269 us
  local copies, waits for them, and re-layouts: 7.09 us -> 34.6 us
  starting transfers between devices: 2.47 us -> 18.5 us
  between operations: 13.5 us -> 0.15 us
    ppermute x0 -> x15, waiting for transfers between devices: none -> 264 us  [the longest x7 211 us: gather_around(): from_right = lax.ppermute(from_right, axis, left)]
    all_gather x1 -> x0, waiting for transfers between devices: 176 us -> none  [on_device(): lax.all_gather(qkv_weight, 'ctx', axis=1, tiled=True)]
    dynamic_update_slice x0 -> x16, local copies, waits for them, and re-layouts: none -> 21.1 us  [the longest x8 10.5 us: gather_around(): lax.dynamic_update_slice_in_dim(out, from_left, (place - step) % size * s...]
    ppermute x0 -> x15, starting transfers between devices: none -> 16.6 us  [the longest x8 10.7 us: gather_around(): from_left = lax.ppermute(from_left, axis, ahead)]
    broadcast_in_dim x0 -> x1, local copies, waits for them, and re-layouts: none -> 6.34 us  [gather_around(): jnp.zeros((*value.shape[:dim], size * span, *value.shape[dim + 1:]), valu...]
  transfers between devices with their start and end apart: 2 -> 16, of which waited for: 2 -> 12; matrix products, arithmetic and copies ran while one was open for 2% -> 9% of each run, Pallas kernels for 0% -> 0%
where the time goes in v1:
time: 352 us; the launch traced here: 351 us
  waiting for transfers between devices  269 us (76%)
  local copies, waits for them, and re-layouts  34.6 us (10%)
  matrix products  18.6 us (5%)
  starting transfers between devices  18.5 us (5%)
  other arithmetic  9.9 us (3%)
    ppermute x7, waiting for transfers between devices, gather_around(): from_right = lax.ppermute(from_right, axis, left)  211 us
    ppermute x8, waiting for transfers between devices, gather_around(): from_left = lax.ppermute(from_left, axis, ahead)  52.9 us
    ppermute x8, starting transfers between devices, gather_around(): from_left = lax.ppermute(from_left, axis, ahead)  10.7 us
    dynamic_update_slice x8, local copies, waits for them, and re-layouts, gather_around(): lax.dynamic_update_slice_in_dim(out, from_left, (place - step) % size * s...  10.5 us
    dynamic_update_slice x7, local copies, waits for them, and re-layouts, gather_around(): lax.dynamic_update_slice_in_dim(out, from_right, (place + step) % size *...  9.59 us
    dot_general x1, matrix products, on_device(): jnp.dot(normed, gather_around(qkv_weight, 'ctx', 1), preferred_element_ty...  9.16 us
  transfers between devices with their start and end apart: 16, of which 12 were waited for; matrix products, arithmetic and copies ran while one was open for 9% of the time, Pallas kernels for 0%

profile of v1, /device:TPU:4, one launch (start us, length us, event | category | flops | bytes accessed | tf_op | source)
XLA Modules:
  0.0 351.2 jit_solution(13714206172110409527)
XLA Ops:
  2.9 22.1 %collective-permute-done = bf16[2880,160]{0,1:T(8,128)(2,1)} collective-permute-done((bf16[2880,160]{0,1:T(8,128)(2,1)}, bf16[2880,160]{0,1:T(8,128)(2,1)}, u32[]{:S(2)}, u32[]{:S(2)}) %collective-permute-start) | collective-permute-done | bytes 921632 | tf_op jit(solution)/shard_map/ppermute | solution.py:21
  25.6 18.8 %collective-permute-done.1 = bf16[2880,160]{0,1:T(8,128)(2,1)} collective-permute-done((bf16[2880,160]{0,1:T(8,128)(2,1)}, bf16[2880,160]{0,1:T(8,128)(2,1)}, u32[]{:S(2)}, u32[]{:S(2)}) %collective-permute-start.1) | collective-permute-done | bytes 921632 | tf_op jit(solution)/shard_map/ppermute | solution.py:26
  44.3 2.3 collective-permute-start.3
  49.2 17.4 %collective-permute-done.2 = bf16[2880,160]{0,1:T(8,128)(2,1)S(1)} collective-permute-done((bf16[2880,160]{0,1:T(8,128)(2,1)}, bf16[2880,160]{0,1:T(8,128)(2,1)S(1)}, u32[]{:S(2)}, u32[]{:S(2)}) %collective-permute-start.2) | collective-permute-done | bytes 921632 | tf_op jit(solution)/shard_map/ppermute | solution.py:21
  68.2 18.0 %collective-permute-done.3 = bf16[2880,160]{0,1:T(8,128)(2,1)S(1)} collective-permute-done((bf16[2880,160]{0,1:T(8,128)(2,1)}, bf16[2880,160]{0,1:T(8,128)(2,1)S(1)}, u32[]{:S(2)}, u32[]{:S(2)}) %collective-permute-start.3) | collective-permute-done | bytes 921632 | tf_op jit(solution)/shard_map/ppermute | solution.py:26
  86.2 2.1 collective-permute-start.5
  88.3 6.3 %broadcast_in_dim.16 = bf16[2880,2560]{0,1:T(8,128)(2,1)} broadcast(bf16[]{:T(256)} %constant.125.clone.1), dimensions={} | broadcast | bytes 14745602 | tf_op jit(solution)/shard_map/broadcast_in_dim | solution.py:16
  95.7 12.9 %collective-permute-done.4 = bf16[2880,160]{0,1:T(8,128)(2,1)} collective-permute-done((bf16[2880,160]{0,1:T(8,128)(2,1)S(1)}, bf16[2880,160]{0,1:T(8,128)(2,1)}, u32[]{:S(2)}, u32[]{:S(2)}) %collective-permute-start.4) | collective-permute-done | bytes 921632 | tf_op jit(solution)/shard_map/ppermute | solution.py:21
  108.6 2.2 constant_dynamic-update-slice_fusion.14
  110.8 37.5 %collective-permute-done.5 = bf16[2880,160]{0,1:T(8,128)(2,1)} collective-permute-done((bf16[2880,160]{0,1:T(8,128)(2,1)S(1)}, bf16[2880,160]{0,1:T(8,128)(2,1)}, u32[]{:S(2)}, u32[]{:S(2)}) %collective-permute-start.5) | collective-permute-done | bytes 921632 | tf_op jit(solution)/shard_map/ppermute | solution.py:26
  148.3 2.2 constant_dynamic-update-slice_fusion.13
  150.5 2.0 collective-permute-start.8
  154.6 35.0 %collective-permute-done.7 = bf16[2880,160]{0,1:T(8,128)(2,1)S(1)} collective-permute-done((bf16[2880,160]{0,1:T(8,128)(2,1)}, bf16[2880,160]{0,1:T(8,128)(2,1)S(1)}, u32[]{:S(2)}, u32[]{:S(2)}) %collective-permute-start.7) | collective-permute-done | bytes 921632 | tf_op jit(solution)/shard_map/ppermute | solution.py:26
  189.6 2.2 constant_dynamic-update-slice_fusion.10
  193.8 2.2 constant_dynamic-update-slice_fusion.9
  197.0 32.5 %collective-permute-done.9 = bf16[2880,160]{0,1:T(8,128)(2,1)S(1)} collective-permute-done((bf16[2880,160]{0,1:T(8,128)(2,1)S(1)}, bf16[2880,160]{0,1:T(8,128)(2,1)S(1)}, u32[]{:S(2)}, u32[]{:S(2)}) %collective-permute-start.9) | collective-permute-done | bytes 921632 | tf_op jit(solution)/shard_map/ppermute | solution.py:26
  231.1 2.5 collective-permute-start.12
  235.7 45.9 %collective-permute-done.11 = bf16[2880,160]{0,1:T(8,128)(2,1)S(1)} collective-permute-done((bf16[2880,160]{0,1:T(8,128)(2,1)S(1)}, bf16[2880,160]{0,1:T(8,128)(2,1)S(1)}, u32[]{:S(2)}, u32[]{:S(2)}) %collective-permute-start.11) | collective-permute-done | bytes 921632 | tf_op jit(solution)/shard_map/ppermute | solution.py:26
  282.6 2.1 collective-permute-start.14
  286.8 23.0 %collective-permute-done.13 = bf16[2880,160]{0,1:T(8,128)(2,1)S(1)} collective-permute-done((bf16[2880,160]{0,1:T(8,128)(2,1)S(1)}, bf16[2880,160]{0,1:T(8,128)(2,1)S(1)}, u32[]{:S(2)}, u32[]{:S(2)}) %collective-permute-start.13) | collective-permute-done | bytes 921632 | tf_op jit(solution)/shard_map/ppermute | solution.py:26
  311.8 9.2 %convolution_add_fusion = f32[256,2560]{1,0:T(8,128)S(1)} fusion(bf16[2880,2560]{0,1:T(8,128)(2,1)} %constant_dynamic-update-slice_fusion, bf16[256,2880]{0,1:T(8,128)(2,1)} %param.10, f32[2880]{0:T(1024)S(1)} %copy-done.1, f32[256]{0:T(256)S(1)} %add_rsqrt_fusion, f32[2560]{0:T(1024)S(1)} %copy-done.2), kind=kOutput, calls=%fused_computation.30 | convolution fusion | flops 3778478080 | bytes 18864384 | tf_op jit(solution)/shard_map/dot_general | solution.py:95
  328.7 5.7 %collective-permute-done.15 = bf16[2,128,256]{2,1,0:T(8,128)(2,1)S(1)} collective-permute-done((bf16[2,128,256]{2,1,0:T(8,128)(2,1)S(1)}, bf16[2,128,256]{2,1,0:T(8,128)(2,1)S(1)}, u32[]{:S(2)}, u32[]{:S(2)}) %collective-permute-start.15) | collective-permute-done | bytes 131104 | tf_op jit(solution)/shard_map/ppermute | solution.py:36
  335.8 13.2 %while.11 = (s32[]{:T(128)}, bf16[4,1,256,8,64]{2,4,3,1,0:T(8,128)(2,1)}, bf16[4,1,384,64]{2,3,1,0:T(8,128)(2,1)S(1)}, bf16[4,1,384,64]{2,3,1,0:T(8,128)(2,1)S(1...) while((s32[]{:T(128)}, ...), condition=%wide.region_4.5_spmd.clone, body=%wide.region_1.4_spmd.clone.sunk | while | flops 211390464 | bytes 10538201 | solution.py:124
  349.0 2.3 copy.26
  (85 shorter events, 44.5 us)
Async XLA Ops:
  0.0 94.6 %copy-start = (bf16[2880,160]{0,1:T(8,128)(2,1)S(1)}, bf16[2880,160]{0,1:T(8,128)(2,1)}, u32[]{:S(2)}) copy-start(bf16[2880,160]{0,1:T(8,128)(2,1)} %param.13) | copy-start | bytes 2764804
  0.0 25.0 %collective-permute-start = (bf16[2880,160]{0,1:T(8,128)(2,1)}, bf16[2880,160]{0,1:T(8,128)(2,1)}, u32[]{:S(2)}, u32[]{:S(2)}) collective-permute-start(bf16[2880,160]{0,1:T(8,128)(2,1)} %param.13), channel_id=1, source_target_pairs={{0,1},{1,2},{2,3},{3,4},{4,5},{5,6},{6,7},{7,8},{8,9},{9,10},{10,1... | collective-permute-start | bytes 2764808 | tf_op jit(solution)/shard_map/ppermute | solution.py:21
  1.5 42.8 %collective-permute-start.1 = (bf16[2880,160]{0,1:T(8,128)(2,1)}, bf16[2880,160]{0,1:T(8,128)(2,1)}, u32[]{:S(2)}, u32[]{:S(2)}) collective-permute-start(bf16[2880,160]{0,1:T(8,128)(2,1)} %param.13), channel_id=1, source_target_pairs={{0,15},{1,0},{2,1},{3,2},{4,3},{5,4},{6,5},{7,6},{8,7},{9,8},{10,9... | collective-permute-start | bytes 2764808 | tf_op jit(solution)/shard_map/ppermute | solution.py:26
  25.0 41.6 %collective-permute-start.2 = (bf16[2880,160]{0,1:T(8,128)(2,1)}, bf16[2880,160]{0,1:T(8,128)(2,1)S(1)}, u32[]{:S(2)}, u32[]{:S(2)}) collective-permute-start(bf16[2880,160]{0,1:T(8,128)(2,1)} %collective-permute-done), channel_id=1, source_target_pairs={{0,1},{1,2},{2,3},{3,4},{4,5},{5,6},{6,7},{7,8},{8,9},{9,10},{10,1... | collective-permute-start | bytes 2764808 | tf_op jit(solution)/shard_map/ppermute | solution.py:21
  44.3 41.8 %collective-permute-start.3 = (bf16[2880,160]{0,1:T(8,128)(2,1)}, bf16[2880,160]{0,1:T(8,128)(2,1)S(1)}, u32[]{:S(2)}, u32[]{:S(2)}) collective-permute-start(bf16[2880,160]{0,1:T(8,128)(2,1)} %collective-permute-done.1), channel_id=1, source_target_pairs={{0,15},{1,0},{2,1},{3,2},{4,3},{5,4},{6,5},{7,6},{8,7},{9,8},{10,9... | collective-permute-start | bytes 2764808 | tf_op jit(solution)/shard_map/ppermute | solution.py:26
  66.6 42.0 %collective-permute-start.4 = (bf16[2880,160]{0,1:T(8,128)(2,1)S(1)}, bf16[2880,160]{0,1:T(8,128)(2,1)}, u32[]{:S(2)}, u32[]{:S(2)}) collective-permute-start(bf16[2880,160]{0,1:T(8,128)(2,1)S(1)} %collective-permute-done.2), channel_id=1, source_target_pairs={{0,1},{1,2},{2,3},{3,4},{4,5},{5,6},{6,7},{7,8},{8,9},{9,10},{10,1... | collective-permute-start | bytes 2764808 | tf_op jit(solution)/shard_map/ppermute | solution.py:21
  86.2 62.2 %collective-permute-start.5 = (bf16[2880,160]{0,1:T(8,128)(2,1)S(1)}, bf16[2880,160]{0,1:T(8,128)(2,1)}, u32[]{:S(2)}, u32[]{:S(2)}) collective-permute-start(bf16[2880,160]{0,1:T(8,128)(2,1)S(1)} %collective-permute-done.3), channel_id=1, source_target_pairs={{0,15},{1,0},{2,1},{3,2},{4,3},{5,4},{6,5},{7,6},{8,7},{9,8},{10,9... | collective-permute-start | bytes 2764808 | tf_op jit(solution)/shard_map/ppermute | solution.py:26
  94.6 217.2 %copy-start.1 = (f32[2880]{0:T(1024)S(1)}, f32[2880]{0:T(1024)}, u32[]{:S(2)}) copy-start(f32[2880]{0:T(1024)} %param.12) | copy-start | bytes 34564
  94.7 217.2 %copy-start.2 = (f32[2560]{0:T(1024)S(1)}, f32[2560]{0:T(1024)}, u32[]{:S(2)}) copy-start(f32[2560]{0:T(1024)} %param.14) | copy-start | bytes 30724
  108.6 41.9 %collective-permute-start.6 = (bf16[2880,160]{0,1:T(8,128)(2,1)}, bf16[2880,160]{0,1:T(8,128)(2,1)S(1)}, u32[]{:S(2)}, u32[]{:S(2)}) collective-permute-start(bf16[2880,160]{0,1:T(8,128)(2,1)} %collective-permute-done.4), channel_id=1, source_target_pairs={{0,1},{1,2},{2,3},{3,4},{4,5},{5,6},{6,7},{7,8},{8,9},{9,10},{10,1... | collective-permute-start | bytes 2764808 | tf_op jit(solution)/shard_map/ppermute | solution.py:21
  148.3 41.3 %collective-permute-start.7 = (bf16[2880,160]{0,1:T(8,128)(2,1)}, bf16[2880,160]{0,1:T(8,128)(2,1)S(1)}, u32[]{:S(2)}, u32[]{:S(2)}) collective-permute-start(bf16[2880,160]{0,1:T(8,128)(2,1)} %collective-permute-done.5), channel_id=1, source_target_pairs={{0,15},{1,0},{2,1},{3,2},{4,3},{5,4},{6,5},{7,6},{8,7},{9,8},{10,9... | collective-permute-start | bytes 2764808 | tf_op jit(solution)/shard_map/ppermute | solution.py:26
  150.5 41.3 %collective-permute-start.8 = (bf16[2880,160]{0,1:T(8,128)(2,1)S(1)}, bf16[2880,160]{0,1:T(8,128)(2,1)S(1)}, u32[]{:S(2)}, u32[]{:S(2)}) collective-permute-start(bf16[2880,160]{0,1:T(8,128)(2,1)S(1)} %collective-permute-done.6), channel_id=1, source_target_pairs={{0,1},{1,2},{2,3},{3,4},{4,5},{5,6},{6,7},{7,8},{8,9},{9,10},{10,1... | collective-permute-start | bytes 2764808 | tf_op jit(solution)/shard_map/ppermute | solution.py:21
  189.6 39.9 %collective-permute-start.9 = (bf16[2880,160]{0,1:T(8,128)(2,1)S(1)}, bf16[2880,160]{0,1:T(8,128)(2,1)S(1)}, u32[]{:S(2)}, u32[]{:S(2)}) collective-permute-start(bf16[2880,160]{0,1:T(8,128)(2,1)S(1)} %collective-permute-done.7), channel_id=1, source_target_pairs={{0,15},{1,0},{2,1},{3,2},{4,3},{5,4},{6,5},{7,6},{8,7},{9,8},{10,9... | collective-permute-start | bytes 2764808 | tf_op jit(solution)/shard_map/ppermute | solution.py:26
  191.8 39.3 %collective-permute-start.10 = (bf16[2880,160]{0,1:T(8,128)(2,1)S(1)}, bf16[2880,160]{0,1:T(8,128)(2,1)S(1)}, u32[]{:S(2)}, u32[]{:S(2)}) collective-permute-start(bf16[2880,160]{0,1:T(8,128)(2,1)S(1)} %collective-permute-done.8), channel_id=1, source_target_pairs={{0,1},{1,2},{2,3},{3,4},{4,5},{5,6},{6,7},{7,8},{8,9},{9,10},{10,1... | collective-permute-start | bytes 2764808 | tf_op jit(solution)/shard_map/ppermute | solution.py:21
  229.5 52.0 %collective-permute-start.11 = (bf16[2880,160]{0,1:T(8,128)(2,1)S(1)}, bf16[2880,160]{0,1:T(8,128)(2,1)S(1)}, u32[]{:S(2)}, u32[]{:S(2)}) collective-permute-start(bf16[2880,160]{0,1:T(8,128)(2,1)S(1)} %collective-permute-done.9), channel_id=1, source_target_pairs={{0,15},{1,0},{2,1},{3,2},{4,3},{5,4},{6,5},{7,6},{8,7},{9,8},{10,9... | collective-permute-start | bytes 2764808 | tf_op jit(solution)/shard_map/ppermute | solution.py:26
  231.1 51.4 %collective-permute-start.12 = (bf16[2880,160]{0,1:T(8,128)(2,1)S(1)}, bf16[2880,160]{0,1:T(8,128)(2,1)S(1)}, u32[]{:S(2)}, u32[]{:S(2)}) collective-permute-start(bf16[2880,160]{0,1:T(8,128)(2,1)S(1)} %collective-permute-done.10), channel_id=1, source_target_pairs={{0,1},{1,2},{2,3},{3,4},{4,5},{5,6},{6,7},{7,8},{8,9},{9,10},{10,1... | collective-permute-start | bytes 2764808 | tf_op jit(solution)/shard_map/ppermute | solution.py:21
  281.6 28.2 %collective-permute-start.13 = (bf16[2880,160]{0,1:T(8,128)(2,1)S(1)}, bf16[2880,160]{0,1:T(8,128)(2,1)S(1)}, u32[]{:S(2)}, u32[]{:S(2)}) collective-permute-start(bf16[2880,160]{0,1:T(8,128)(2,1)S(1)} %collective-permute-done.11), channel_id=1, source_target_pairs={{0,15},{1,0},{2,1},{3,2},{4,3},{5,4},{6,5},{7,6},{8,7},{9,8},{10,9... | collective-permute-start | bytes 2764808 | tf_op jit(solution)/shard_map/ppermute | solution.py:26
  282.6 28.2 %collective-permute-start.14 = (bf16[2880,160]{0,1:T(8,128)(2,1)S(1)}, bf16[2880,160]{0,1:T(8,128)(2,1)S(1)}, u32[]{:S(2)}, u32[]{:S(2)}) collective-permute-start(bf16[2880,160]{0,1:T(8,128)(2,1)S(1)} %collective-permute-done.12), channel_id=1, source_target_pairs={{0,1},{1,2},{2,3},{3,4},{4,5},{5,6},{6,7},{7,8},{8,9},{9,10},{10,1... | collective-permute-start | bytes 2764808 | tf_op jit(solution)/shard_map/ppermute | solution.py:21
  326.7 7.8 %collective-permute-start.15 = (bf16[2,128,256]{2,1,0:T(8,128)(2,1)S(1)}, bf16[2,128,256]{2,1,0:T(8,128)(2,1)S(1)}, u32[]{:S(2)}, u32[]{:S(2)}) collective-permute-start(bf16[2,128,256]{2,1,0:T(8,128)(2,1)S(1)} %pad_maximum_fusion), channel_id=1, source_target_pairs={{0,1},{1,2},{2,3},{3,4},{4,5},{5,6},{6,7},{7,8},{8,9},{9,10},{10,1... | collective-permute-start | bytes 393224 | tf_op jit(solution)/shard_map/ppermute | solution.py:36
